TPU v7x, 256 devices: a whole 4x4x8 slice. The times are simulated.
256 devices in a mesh: section: 4 (over x), shard: 16 (over z, core), tensor: 4 (over y).
Axes of the slice: x: 4, y: 4, z: 8, core: 2. Of those that a mesh axis runs over, the one named last changes fastest.
Arguments:
- grad_terms: float32 [4, 16, 5120, 1280], P('section', 'shard', 'tensor'), may hold values from -5 to 5
- weights: bfloat16 [4, 4, 1280, 1280], P('section', 'tensor', 'shard'), may hold values from -4 to 4
- basis: float32 [4, 1280, 256], P('section'), may hold values from -5 to 5
- first_moment: float32 [4, 4, 1280, 256], P('section', 'tensor', 'shard'), may hold values from -4 to 4
- second_moment: float32 [4, 4, 1280, 256], P('section', 'tensor', 'shard'), may hold values from 0.1 to 2
Outputs:
- new_weights: bfloat16 [4, 4, 1280, 1280], P('section', 'tensor', 'shard')
- new_first: float32 [4, 4, 1280, 256], P('section', 'tensor', 'shard')
- new_second: float32 [4, 4, 1280, 256], P('section', 'tensor', 'shard')
- new_basis: float32 [4, 1280, 256], P('section')
All inputs are finite; a program needn't handle non-finite values.
Results may differ from a plain program's by a relative error of at most 0.001.
Values sent between devices are 32-bit elements; how exact they have to be, the bound alone decides.
No kernel may reach another device: no remote copies, remote signals or barrier semaphores. Data moves between devices by JAX's collectives and lax.ppermute only.
A program may use at most 64 MiB of HBM per device.

v0:
```python
import math
import jax
import jax.numpy as jnp
from jax import lax
from jax.sharding import PartitionSpec as P

NS_STEPS = 5


def matmul(left, right):
    return jnp.dot(left, right, precision=lax.Precision.HIGHEST, preferred_element_type=jnp.float32)


def inner_rows(left, right):
    return lax.dot_general(
        left,
        right,
        (((0,), (0,)), ((), ())),
        precision=lax.Precision.HIGHEST,
        preferred_element_type=jnp.float32,
    )


def local_gram(iterate):
    return inner_rows(iterate, iterate)


def newton_steps(power_part, gram_fn):
    gram_now = gram_fn(power_part)
    scaling = lax.rsqrt(jnp.trace(gram_now) + 1e-06)
    iterate = power_part * scaling
    gram_now = gram_now * (scaling * scaling)
    for sweep in range(NS_STEPS):
        iterate = 1.5 * iterate - 0.5 * matmul(iterate, gram_now)
        if sweep + 1 < NS_STEPS:
            gram_now = gram_fn(iterate)
    return iterate


def per_device(grad_terms, weights, basis, first_moment, second_moment):
    gradient = grad_terms[0, 0]
    basis_now = basis[0]
    root_width = math.sqrt(basis_now.shape[0])
    rows = first_moment.shape[2]
    low_rank = (
        lax.psum_scatter(matmul(gradient, basis_now), "shard", scatter_dimension=0, tiled=True)
        / root_width
    )
    low_rank_block = lax.all_gather(low_rank, "shard", axis=0, tiled=True)
    power_part = inner_rows(gradient, low_rank_block)
    flat = power_part.reshape(-1, 640)
    power_rows = lax.psum_scatter(flat, "shard", scatter_dimension=0, tiled=True)
    power_rows = lax.psum_scatter(power_rows, "tensor", scatter_dimension=0, tiled=True)
    power_rows = lax.all_gather(power_rows, "tensor", axis=0, tiled=True)
    power = lax.all_gather(power_rows, "shard", axis=0, tiled=True).reshape(power_part.shape)
    moment_one = 0.9 * first_moment[0, 0] + 0.1 * low_rank
    moment_two = 0.95 * second_moment[0, 0] + 0.05 * low_rank * low_rank
    direction = moment_one / (jnp.sqrt(moment_two) + 1e-08)
    update = lax.dot_general(
        direction,
        basis_now,
        (((1,), (1,)), ((), ())),
        precision=lax.Precision.HIGHEST,
        preferred_element_type=jnp.float32,
    )
    stepped = weights[0, 0].astype(jnp.float32) - 0.5 * update / root_width
    normed = stepped * lax.rsqrt(jnp.mean(stepped * stepped, axis=1, keepdims=True) + 1e-06)
    new_weights = normed.astype(jnp.bfloat16)
    iterate = newton_steps(power, local_gram)
    new_basis = iterate * root_width
    return (
        new_weights[None, None],
        moment_one[None, None],
        moment_two[None, None],
        new_basis[None],
    )


def solution(mesh):
    return jax.shard_map(
        per_device,
        mesh=mesh,
        in_specs=(
            P("section", "shard", "tensor", None),
            P("section", "tensor", "shard", None),
            P("section", None, None),
            P("section", "tensor", "shard", None),
            P("section", "tensor", "shard", None),
        ),
        out_specs=(
            P("section", "tensor", "shard", None),
            P("section", "tensor", "shard", None),
            P("section", "tensor", "shard", None),
            P("section", None, None),
        ),
        check_vma=False,
    )
```

profile of v0, /device:TPU:1, one launch (start us, length us, event | category | flops | bytes accessed | tf_op | source)
XLA Modules:
  0.0 317.3 jit_solution(8690136283710917015)
XLA Ops:
  7.2 0.0 copy-start
  7.2 0.0 reduce-scatter.3.cloned.1.call-start
  7.2 1.3 copy-done
  8.5 8.2 %fusion.2 = f32[1280,256]{1,0:T(8,128)} fusion(f32[1,1,1280,1280]{3,2,1,0:T(8,128)} %param.5, f32[1,1280,256]{2,1,0:T(8,128)S(1)} %copy-done), kind=kOutput, calls=%fused_computation.2 | convolution fusion | flops 5033164800 | bytes 9175040 | tf_op jit(solution)/shard_map/dot_general | solution.py:11
  16.7 0.0 copy-start.1
  16.7 0.0 copy-start.2
  16.7 0.0 reduce-scatter.3.cloned.1.call-update
  16.7 0.0 all-gather.3.cloned.1.call-start
  16.8 59.8 %reduce-scatter.3.cloned.1.call-done = f32[80,256]{1,0:T(8,128)} async-done(((f32[1280,256]{1,0:T(8,128)}), f32[80,256]{1,0:T(8,128)}) %reduce-scatter.3.cloned.1.call-update) | async-done | bytes 81936 | tf_op jit(solution)/shard_map/reduce_scatter | solution.py:46
  76.5 0.0 copy-done.1
  76.5 0.0 copy-done.2
  76.5 1.6 broadcast_multiply_fusion
  78.1 0.0 all-gather.3.cloned.1.call-update
  78.2 0.0 reduce-scatter.5.cloned.1.call-start
  78.2 41.1 %all-gather.3.cloned.1.call-done = f32[1280,256]{1,0:T(8,128)} async-done(((f32[80,256]{1,0:T(8,128)}), f32[1280,256]{1,0:T(8,128)}) %all-gather.3.cloned.1.call-update) | async-done | bytes 1310736 | tf_op jit(solution)/shard_map/all_gather | solution.py:49
  119.3 8.9 %fusion.11 = f32[1280,256]{0,1:T(8,128)S(1)} fusion(f32[1280,256]{1,0:T(8,128)} %all-gather.3.cloned.1.call-done, f32[1,1,1280,1280]{3,2,1,0:T(8,128)} %param.5), kind=kOutput, calls=%fused_computation.16 | convolution fusion | flops 5033164800 | bytes 9175040 | tf_op jit(solution)/shard_map/dot_general | solution.py:15
  128.2 1.5 copy.10
  129.7 2.6 reshape.28
  132.3 0.0 copy-start.5
  132.3 0.0 copy-start.3
  132.3 0.0 copy-start.4
  132.3 0.0 reduce-scatter.5.cloned.1.call-update
  132.3 0.0 all-reduce.3.cloned.1.call-start
  132.4 53.9 %reduce-scatter.5.cloned.1.call-done = f32[32,640]{1,0:T(8,128)} async-done(((f32[512,640]{1,0:T(8,128)}), f32[32,640]{1,0:T(8,128)}) %reduce-scatter.5.cloned.1.call-update) | async-done | bytes 81936 | tf_op jit(solution)/shard_map/reduce_scatter | solution.py:52
  186.3 0.0 all-reduce.3.cloned.1.call-update
  186.3 0.0 all-gather.5.cloned.1.call-start
  186.3 0.0 copy-done.5
  186.4 0.6 dynamic-slice
  187.6 46.0 %all-reduce.3.cloned.1.call-done = f32[32,640]{1,0:T(8,128)} async-done(((f32[32,640]{1,0:T(8,128)}), f32[32,640]{1,0:T(8,128)}) %all-reduce.3.cloned.1.call-update) | async-done | bytes 81936
  233.6 0.7 constant_dynamic-slice_fusion
  234.3 9.7 %all_gather.10 = f32[32,640]{1,0:T(8,128)} all-gather(f32[8,640]{1,0:T(8,128)S(1)} %constant_dynamic-slice_fusion), channel_id=1, replica_groups=mesh['section'=4,'shard'=16,'tensor'=4] {'tensor'}, dimensions={0}, use_global_device_ids=true | all-gather | bytes 102400 | tf_op jit(solution)/shard_map/all_gather | solution.py:54
  244.1 0.0 all-gather.5.cloned.1.call-update
  244.1 0.0 copy-done.3
  244.1 0.0 copy-done.4
  244.1 1.5 multiply_reduce_fusion
  245.6 0.8 fusion.20
  246.4 42.6 %all-gather.5.cloned.1.call-done = f32[512,640]{1,0:T(8,128)} async-done(((f32[32,640]{1,0:T(8,128)}), f32[512,640]{1,0:T(8,128)}) %all-gather.5.cloned.1.call-update) | async-done | bytes 1310736 | tf_op jit(solution)/shard_map/all_gather | solution.py:55
  289.0 1.8 reshape.29
  290.9 2.9 select_reduce_fusion
  294.4 1.2 fusion.9
  295.6 2.2 fusion.34
  297.9 1.2 fusion.8
  299.1 2.2 fusion.35
  301.3 1.2 fusion.7
  302.5 2.5 fusion.36
  305.0 1.2 fusion.6
  306.2 2.2 fusion.37
  308.5 2.3 fusion.10
  (1 shorter events, 0.0 us)
Async XLA Ops:
  7.2 1.3 copy-start
  7.2 69.4 %reduce-scatter.3.cloned.1.call-start = ((), (), s32[]{:S(2)}) async-start(), calls=%async_computation.2 | async-start | bytes 1392640 | tf_op jit(solution)/shard_map/reduce_scatter | solution.py:46
  16.7 59.8 %copy-start.1 = (f32[1,1,80,256]{3,2,1,0:T(8,128)S(1)}, f32[1,1,80,256]{3,2,1,0:T(8,128)}, u32[]{:S(2)}) copy-start(f32[1,1,80,256]{3,2,1,0:T(8,128)} %param.8) | copy-start | bytes 245764
  16.7 59.8 %copy-start.2 = (f32[1,1,80,256]{3,2,1,0:T(8,128)S(1)}, f32[1,1,80,256]{3,2,1,0:T(8,128)}, u32[]{:S(2)}) copy-start(f32[1,1,80,256]{3,2,1,0:T(8,128)} %param.9) | copy-start | bytes 245764
  16.7 102.6 %all-gather.3.cloned.1.call-start = ((), (), s32[]{:S(2)}) async-start(), calls=%async_computation.3 | async-start | bytes 1392640 | tf_op jit(solution)/shard_map/all_gather | solution.py:49
  78.2 108.1 %reduce-scatter.5.cloned.1.call-start = ((), (), s32[]{:S(2)}) async-start(), calls=%async_computation.4 | async-start | bytes 1392640 | tf_op jit(solution)/shard_map/reduce_scatter | solution.py:52
  132.3 54.0 %copy-start.5 = (u32[256]{0:T(256)S(1)}, u32[256]{0:T(256)}, u32[]{:S(2)}) copy-start(u32[256]{0:T(256)} %constant.45) | copy-start | bytes 3076
  132.3 111.8 %copy-start.3 = (f32[80,256]{1,0:T(8,128)S(1)}, f32[80,256]{1,0:T(8,128)}, u32[]{:S(2)}) copy-start(f32[80,256]{1,0:T(8,128)} %reduce-scatter.3.cloned.1.call-done) | copy-start | bytes 245764
  132.3 111.8 %copy-start.4 = (bf16[1,1,80,1280]{3,2,1,0:T(8,128)(2,1)S(1)}, bf16[1,1,80,1280]{3,2,1,0:T(8,128)(2,1)}, u32[]{:S(2)}) copy-start(bf16[1,1,80,1280]{3,2,1,0:T(8,128)(2,1)} %param.6) | copy-start | bytes 614404
  132.3 101.3 %all-reduce.3.cloned.1.call-start = ((), (), s32[]{:S(2)}) async-start(), calls=%async_computation.6 | async-start | bytes 163840
  186.3 102.7 %all-gather.5.cloned.1.call-start = ((), (), s32[]{:S(2)}) async-start(), calls=%async_computation.5 | async-start | bytes 1392640 | tf_op jit(solution)/shard_map/all_gather | solution.py:55
Sparse Core Ops, SparseCore 0:
  16.8 59.6 reduce-scatter.2
  78.9 40.3 all-gather.2
  132.5 53.7 reduce-scatter.4
  188.4 45.1 all-reduce.2
  244.2 44.7 all-gather.4
where the time goes:
time: 318 us; the launch traced here: 317 us
  waiting for transfers between devices  244 us (77%)
  matrix products  37.7 us (12%)
  between operations  15.2 us (5%)
  blocking collectives  9.73 us (3%)
  local copies, waits for them, and re-layouts  8.53 us (3%)
    reduce_scatter x1, waiting for transfers between devices, per_device(): lax.psum_scatter(matmul(gradient, basis_now), 'shard', scatter_dimension=...  59.8 us
    reduce_scatter x1, waiting for transfers between devices, per_device(): lax.psum_scatter(flat, 'shard', scatter_dimension=0, tiled=True)  53.9 us
    unnamed x6, waiting for transfers between devices  46.1 us
    all_gather x1, waiting for transfers between devices, per_device(): lax.all_gather(power_rows, 'shard', axis=0, tiled=True)  42.6 us
    all_gather x1, waiting for transfers between devices, per_device(): low_rank_block = lax.all_gather(low_rank, 'shard', axis=0, tiled=True)  41.1 us
    dot_general x6, matrix products, inner_rows(): lax.dot_general(left, right, (((0,), (0,)), ((), ())), precision=lax.Prec...  20.9 us
    dot_general x6, matrix products, matmul(): jnp.dot(left, right, precision=lax.Precision.HIGHEST, preferred_element_t...  15.3 us
    all_gather x1, blocking collectives, per_device(): power_rows = lax.all_gather(power_rows, 'tensor', axis=0, tiled=True)  9.73 us
  transfers between devices with their start and end apart: 5, of which 5 were waited for; matrix products, arithmetic and copies ran while one was open for 1% of the time, Pallas kernels for 0%

commit v1 on v0

--- a/solution.py
+++ b/solution.py
@@ -51,7 +51,8 @@
     flat = power_part.reshape(-1, 640)
     power_rows = lax.psum_scatter(flat, "shard", scatter_dimension=0, tiled=True)
     power_rows = lax.psum_scatter(power_rows, "tensor", scatter_dimension=0, tiled=True)
-    power_rows = lax.all_gather(power_rows, "tensor", axis=0, tiled=True)
+    copies = jnp.concatenate([power_rows] * lax.axis_size("tensor"), axis=0)
+    power_rows = lax.all_to_all(copies, "tensor", 0, 0, tiled=True)
     power = lax.all_gather(power_rows, "shard", axis=0, tiled=True).reshape(power_part.shape)
     moment_one = 0.9 * first_moment[0, 0] + 0.1 * low_rank
     moment_two = 0.95 * second_moment[0, 0] + 0.05 * low_rank * low_rank

time: 318 us -> 313 us (0.984)
    all_gather x1 -> x0, blocking collectives: 9.73 us -> none  [per_device(): power_rows = lax.all_gather(power_rows, 'tensor', axis=0, tiled=True)]
    all_to_all x0 -> x1, blocking collectives: none -> 7.95 us  [per_device(): power_rows = lax.all_to_all(copies, 'tensor', 0, 0, tiled=True)]
where the time goes in v1:
time: 313 us
  waiting for transfers between devices  241 us (77%)
  matrix products  37.7 us (12%)
  between operations  15.2 us (5%)
  local copies, waits for them, and re-layouts  8.53 us (3%)
  blocking collectives  7.95 us (3%)
    reduce_scatter x1, waiting for transfers between devices, per_device(): lax.psum_scatter(matmul(gradient, basis_now), 'shard', scatter_dimension=...  59.8 us
    reduce_scatter x1, waiting for transfers between devices, per_device(): lax.psum_scatter(flat, 'shard', scatter_dimension=0, tiled=True)  53.9 us
    unnamed x6, waiting for transfers between devices  46.1 us
    all_gather x1, waiting for transfers between devices, per_device(): low_rank_block = lax.all_gather(low_rank, 'shard', axis=0, tiled=True)  41.1 us
    all_gather x1, waiting for transfers between devices, per_device(): lax.all_gather(power_rows, 'shard', axis=0, tiled=True)  39.9 us
    dot_general x6, matrix products, inner_rows(): lax.dot_general(left, right, (((0,), (0,)), ((), ())), precision=lax.Prec...  20.9 us
    dot_general x6, matrix products, matmul(): jnp.dot(left, right, precision=lax.Precision.HIGHEST, preferred_element_t...  15.3 us
    all_to_all x1, blocking collectives, per_device(): power_rows = lax.all_to_all(copies, 'tensor', 0, 0, tiled=True)  7.95 us
  transfers between devices with their start and end apart: 5, of which 5 were waited for; matrix products, arithmetic and copies ran while one was open for 1% of the time, Pallas kernels for 0%

profile of v1, /device:TPU:1, one launch (start us, length us, event | category | flops | bytes accessed | tf_op | source)
XLA Modules:
  0.0 312.7 jit_solution(1135782966647711081)
XLA Ops:
  7.2 0.0 copy-start
  7.2 0.0 reduce-scatter.3.cloned.1.call-start
  7.2 1.3 copy-done
  8.5 8.2 %fusion.2 = f32[1280,256]{1,0:T(8,128)} fusion(f32[1,1,1280,1280]{3,2,1,0:T(8,128)} %param.5, f32[1,1280,256]{2,1,0:T(8,128)S(1)} %copy-done), kind=kOutput, calls=%fused_computation.2 | convolution fusion | flops 5033164800 | bytes 9175040 | tf_op jit(solution)/shard_map/dot_general | solution.py:11
  16.7 0.0 copy-start.1
  16.7 0.0 copy-start.2
  16.7 0.0 reduce-scatter.3.cloned.1.call-update
  16.7 0.0 all-gather.3.cloned.1.call-start
  16.8 59.8 %reduce-scatter.3.cloned.1.call-done = f32[80,256]{1,0:T(8,128)} async-done(((f32[1280,256]{1,0:T(8,128)}), f32[80,256]{1,0:T(8,128)}) %reduce-scatter.3.cloned.1.call-update) | async-done | bytes 81936 | tf_op jit(solution)/shard_map/reduce_scatter | solution.py:46
  76.5 0.0 copy-done.1
  76.5 0.0 copy-done.2
  76.5 1.6 broadcast_multiply_fusion
  78.1 0.0 all-gather.3.cloned.1.call-update
  78.2 0.0 reduce-scatter.5.cloned.1.call-start
  78.2 41.1 %all-gather.3.cloned.1.call-done = f32[1280,256]{1,0:T(8,128)} async-done(((f32[80,256]{1,0:T(8,128)}), f32[1280,256]{1,0:T(8,128)}) %all-gather.3.cloned.1.call-update) | async-done | bytes 1310736 | tf_op jit(solution)/shard_map/all_gather | solution.py:49
  119.3 8.9 %fusion.11 = f32[1280,256]{0,1:T(8,128)S(1)} fusion(f32[1280,256]{1,0:T(8,128)} %all-gather.3.cloned.1.call-done, f32[1,1,1280,1280]{3,2,1,0:T(8,128)} %param.5), kind=kOutput, calls=%fused_computation.16 | convolution fusion | flops 5033164800 | bytes 9175040 | tf_op jit(solution)/shard_map/dot_general | solution.py:15
  128.2 1.5 copy.10
  129.7 2.6 reshape.30
  132.3 0.0 copy-start.5
  132.3 0.0 copy-start.3
  132.3 0.0 copy-start.4
  132.3 0.0 reduce-scatter.5.cloned.1.call-update
  132.3 0.0 all-reduce.3.cloned.1.call-start
  132.4 53.9 %reduce-scatter.5.cloned.1.call-done = f32[32,640]{1,0:T(8,128)} async-done(((f32[512,640]{1,0:T(8,128)}), f32[32,640]{1,0:T(8,128)}) %reduce-scatter.5.cloned.1.call-update) | async-done | bytes 81936 | tf_op jit(solution)/shard_map/reduce_scatter | solution.py:52
  186.3 0.0 all-reduce.3.cloned.1.call-update
  186.3 0.0 all-gather.5.cloned.1.call-start
  186.3 0.0 copy-done.5
  186.4 0.6 dynamic-slice
  187.6 46.0 %all-reduce.3.cloned.1.call-done = f32[32,640]{1,0:T(8,128)} async-done(((f32[32,640]{1,0:T(8,128)}), f32[32,640]{1,0:T(8,128)}) %all-reduce.3.cloned.1.call-update) | async-done | bytes 81936
  233.6 0.7 constant_dynamic-slice_fusion
  234.4 8.0 %all_to_all.12 = f32[4,8,640]{2,1,0:T(8,128)} all-to-all(f32[4,8,640]{2,1,0:T(8,128)S(1)} %maximum_bitcast_fusion), channel_id=1, replica_groups=mesh['section'=4,'shard'=16,'tensor'=4] {'tensor'}, dimensions={0} | all-to-all | bytes 163840 | tf_op jit(solution)/shard_map/all_to_all | solution.py:55
  242.3 0.0 all-gather.5.cloned.1.call-update
  242.3 0.0 copy-done.3
  242.3 0.0 copy-done.4
  242.3 1.5 multiply_reduce_fusion
  243.8 0.8 fusion.20
  244.6 39.9 %all-gather.5.cloned.1.call-done = f32[512,640]{1,0:T(8,128)} async-done(((f32[32,640]{1,0:T(8,128)}), f32[512,640]{1,0:T(8,128)}) %all-gather.5.cloned.1.call-update) | async-done | bytes 1310736 | tf_op jit(solution)/shard_map/all_gather | solution.py:56
  284.5 1.8 reshape.31
  286.3 2.9 select_reduce_fusion
  289.9 1.2 fusion.9
  291.1 2.2 fusion.34
  293.3 1.2 fusion.8
  294.5 2.2 fusion.35
  296.8 1.2 fusion.7
  298.0 2.5 fusion.36
  300.5 1.2 fusion.6
  301.7 2.2 fusion.37
  303.9 2.3 fusion.10
  (2 shorter events, 0.0 us)
Async XLA Ops:
  7.2 1.3 copy-start
  7.2 69.4 %reduce-scatter.3.cloned.1.call-start = ((), (), s32[]{:S(2)}) async-start(), calls=%async_computation.3 | async-start | bytes 1392640 | tf_op jit(solution)/shard_map/reduce_scatter | solution.py:46
  16.7 59.8 %copy-start.1 = (f32[1,1,80,256]{3,2,1,0:T(8,128)S(1)}, f32[1,1,80,256]{3,2,1,0:T(8,128)}, u32[]{:S(2)}) copy-start(f32[1,1,80,256]{3,2,1,0:T(8,128)} %param.8) | copy-start | bytes 245764
  16.7 59.8 %copy-start.2 = (f32[1,1,80,256]{3,2,1,0:T(8,128)S(1)}, f32[1,1,80,256]{3,2,1,0:T(8,128)}, u32[]{:S(2)}) copy-start(f32[1,1,80,256]{3,2,1,0:T(8,128)} %param.9) | copy-start | bytes 245764
  16.7 102.6 %all-gather.3.cloned.1.call-start = ((), (), s32[]{:S(2)}) async-start(), calls=%async_computation.4 | async-start | bytes 1392640 | tf_op jit(solution)/shard_map/all_gather | solution.py:49
  78.2 108.1 %reduce-scatter.5.cloned.1.call-start = ((), (), s32[]{:S(2)}) async-start(), calls=%async_computation.5 | async-start | bytes 1392640 | tf_op jit(solution)/shard_map/reduce_scatter | solution.py:52
  132.3 54.0 %copy-start.5 = (u32[256]{0:T(256)S(1)}, u32[256]{0:T(256)}, u32[]{:S(2)}) copy-start(u32[256]{0:T(256)} %constant.45) | copy-start | bytes 3076
  132.3 110.0 %copy-start.3 = (f32[80,256]{1,0:T(8,128)S(1)}, f32[80,256]{1,0:T(8,128)}, u32[]{:S(2)}) copy-start(f32[80,256]{1,0:T(8,128)} %reduce-scatter.3.cloned.1.call-done) | copy-start | bytes 245764
  132.3 110.0 %copy-start.4 = (bf16[1,1,80,1280]{3,2,1,0:T(8,128)(2,1)S(1)}, bf16[1,1,80,1280]{3,2,1,0:T(8,128)(2,1)}, u32[]{:S(2)}) copy-start(bf16[1,1,80,1280]{3,2,1,0:T(8,128)(2,1)} %param.6) | copy-start | bytes 614404
  132.3 101.3 %all-reduce.3.cloned.1.call-start = ((), (), s32[]{:S(2)}) async-start(), calls=%async_computation.7 | async-start | bytes 163840
  186.3 98.2 %all-gather.5.cloned.1.call-start = ((), (), s32[]{:S(2)}) async-start(), calls=%async_computation.6 | async-start | bytes 1392640 | tf_op jit(solution)/shard_map/all_gather | solution.py:56
Sparse Core Ops, SparseCore 0:
  16.8 59.6 reduce-scatter.2
  78.9 40.3 all-gather.2
  132.5 53.7 reduce-scatter.4
  188.4 45.1 all-reduce.2
  242.4 41.9 all-gather.4
